TPU v7x, 128 devices: a whole 4x4x4 slice. The times are simulated.
128 devices in a mesh: dp: 8 (over x, core), pair: 16 (over z, y).
Axes of the slice: x: 4, y: 4, z: 4, core: 2. Of those that a mesh axis runs over, the one named last changes fastest.
Arguments:
- anchor: bfloat16 [5, 4096, 1024], P(None, ('dp', 'pair')), may hold values from -20 to 20
- partner: bfloat16 [5, 4096, 1024], P(None, ('dp', 'pair')), may hold values from -12 to 12
- counts: int32 [5], replicated, may hold values from 512 to 4096, as said below
- pair_scale: float32 [5], replicated, may hold values from 2 to 8
Outputs:
- loss_value: float32 [], replicated
- grad_anchor: float32 [5, 4096, 1024], P(None, ('dp', 'pair'))
- grad_partner: float32 [5, 4096, 1024], P(None, ('dp', 'pair'))
Inputs may be any that keep to these rules, and one draw needn't show every extreme that they name: The valid samples of pair p are its rows 0 to counts[p] - 1; one pair has all 4096 rows valid.
All inputs are finite; a program needn't handle non-finite values.
Results may differ from a plain program's by a relative error of at most 0.0021.
Values may be sent and summed in bfloat16 or wider, within the bound.
No kernel may reach another device: no remote copies, remote signals or barrier semaphores. Data moves between devices by JAX's collectives and lax.ppermute only.
A program may use at most 128 MiB of HBM per device.

v0:
```python
import math
import jax
import jax.numpy as jnp
from jax import lax
from jax.sharding import PartitionSpec as P

NEG = -1e30


def joined(part, axis, combine):
    gathered = jax.tree.map(lambda a: lax.all_gather(a, axis), part)

    def take(source):
        return jax.tree.map(lambda a: lax.dynamic_index_in_dim(a, source, 0, False), gathered)

    return lax.fori_loop(
        1, lax.axis_size(axis), lambda source, state: combine(state, take(source)), take(0)
    )


def merge_stats(earlier, later):
    highest = jnp.maximum(earlier[0], later[0])
    summed = earlier[1] * jnp.exp(earlier[0] - highest) + later[1] * jnp.exp(later[0] - highest)
    return (highest, summed)


def block_scores(anchor_block, partner_rows, block_valid, col_valid, score_scale):
    scores = (
        jnp.einsum("rd,cd->rc", anchor_block, partner_rows, preferred_element_type=jnp.float32)
        * score_scale
    )
    inside = block_valid[:, None] & col_valid[None, :]
    return (scores, inside)


def local_stats(row_set, col_set, row_global, col_valid, counts, score_scale, tile_rows):
    pair_count = row_set.shape[0]
    total_rows = row_set.shape[1]
    block_count = total_rows // tile_rows
    col_width = col_set.shape[1]
    row_highs, row_sums, col_highs, col_sums = ([], [], [], [])
    for pair_number in range(pair_count):
        anchor_rows = row_set[pair_number]
        partner_rows = col_set[pair_number]
        valid_count = counts[pair_number]
        pair_cols = col_valid[pair_number]

        def local_visit_block(block_index, running):
            high_all, sum_all, col_high, col_sum = running
            start_row = block_index * tile_rows
            block_global = lax.dynamic_slice_in_dim(row_global, start_row, tile_rows, 0)

            def local_live_block(unused):
                anchor_block = lax.dynamic_slice_in_dim(anchor_rows, start_row, tile_rows, 0)
                scores, inside = block_scores(
                    anchor_block, partner_rows, block_global < valid_count, pair_cols, score_scale
                )
                masked = jnp.where(inside, scores, NEG)
                row_high = jnp.max(masked, axis=1)
                row_sum = jnp.sum(
                    jnp.where(inside, jnp.exp(masked - row_high[:, None]), 0.0), axis=1
                )
                block_high = jnp.max(masked, axis=0)
                block_sum = jnp.sum(
                    jnp.where(inside, jnp.exp(masked - block_high[None, :]), 0.0), axis=0
                )
                return (row_high, row_sum, block_high, block_sum)

            def local_empty_block(unused):
                return (
                    jnp.full((tile_rows,), NEG, jnp.float32),
                    jnp.zeros((tile_rows,), jnp.float32),
                    jnp.full((col_width,), NEG, jnp.float32),
                    jnp.zeros((col_width,), jnp.float32),
                )

            row_high, row_sum, block_high, block_sum = lax.cond(
                block_global[0] < valid_count, local_live_block, local_empty_block, 0
            )
            high_all = lax.dynamic_update_slice_in_dim(high_all, row_high, start_row, 0)
            sum_all = lax.dynamic_update_slice_in_dim(sum_all, row_sum, start_row, 0)
            col_high, col_sum = merge_stats((col_high, col_sum), (block_high, block_sum))
            return (high_all, sum_all, col_high, col_sum)

        initial = (
            jnp.full((total_rows,), NEG, jnp.float32),
            jnp.zeros((total_rows,), jnp.float32),
            jnp.full((col_width,), NEG, jnp.float32),
            jnp.zeros((col_width,), jnp.float32),
        )
        high_all, sum_all, col_high, col_sum = lax.fori_loop(
            0, block_count, local_visit_block, initial
        )
        row_highs.append(high_all)
        row_sums.append(sum_all)
        col_highs.append(col_high)
        col_sums.append(col_sum)
    return (jnp.stack(row_highs), jnp.stack(row_sums), jnp.stack(col_highs), jnp.stack(col_sums))


def pair_partials(
    anchor_rows,
    partner_rows,
    row_global,
    pair_cols,
    valid_count,
    row_lse,
    col_lse,
    scale_value,
    score_scale,
    tile_rows,
):
    total_rows = anchor_rows.shape[0]
    block_count = total_rows // tile_rows
    model_width = anchor_rows.shape[1]
    col_width = partner_rows.shape[0]

    def pair_visit_block(block_index, running):
        grad_rows, grad_cols = running
        start_row = block_index * tile_rows
        block_global = lax.dynamic_slice_in_dim(row_global, start_row, tile_rows, 0)

        def pair_live_block(unused):
            anchor_block = lax.dynamic_slice_in_dim(anchor_rows, start_row, tile_rows, 0)
            scores, inside = block_scores(
                anchor_block, partner_rows, block_global < valid_count, pair_cols, score_scale
            )
            block_lse = lax.dynamic_slice_in_dim(row_lse, start_row, tile_rows, 0)
            prob_row = jnp.where(inside, jnp.exp(scores - block_lse[:, None]), 0.0)
            prob_col = jnp.where(inside, jnp.exp(scores - col_lse[None, :]), 0.0)
            weights = (scale_value * 0.5 * (prob_row + prob_col)).astype(jnp.bfloat16)
            part_rows = (
                jnp.dot(weights, partner_rows, preferred_element_type=jnp.float32) * score_scale
            )
            part_cols = (
                jnp.einsum("rc,rd->cd", weights, anchor_block, preferred_element_type=jnp.float32)
                * score_scale
            )
            return (part_rows, part_cols)

        def pair_empty_block(unused):
            return (
                jnp.zeros((tile_rows, model_width), jnp.float32),
                jnp.zeros((col_width, model_width), jnp.float32),
            )

        part_rows, part_cols = lax.cond(
            block_global[0] < valid_count, pair_live_block, pair_empty_block, 0
        )
        grad_rows = lax.dynamic_update_slice_in_dim(grad_rows, part_rows, start_row, 0)
        return (grad_rows, grad_cols + part_cols)

    initial = (
        jnp.zeros((total_rows, model_width), jnp.float32),
        jnp.zeros((col_width, model_width), jnp.float32),
    )
    return lax.fori_loop(0, block_count, pair_visit_block, initial)


def per_device(anchor, partner, counts, pair_scale):
    pair_count, shard_rows, model_width = anchor.shape
    score_scale = 4.0 / math.sqrt(model_width)
    dp_size = lax.axis_size("dp")
    pair_size = lax.axis_size("pair")
    dp_index = lax.axis_index("dp")
    pair_place = lax.axis_index("pair")
    own_first = (dp_index * pair_size + pair_place) * shard_rows
    row_set = lax.all_gather(anchor, "pair", axis=1, tiled=True)
    col_set = lax.all_gather(partner, "dp", axis=1, tiled=True)
    row_first = (dp_index * pair_size + jnp.arange(pair_size, dtype=jnp.int32)) * shard_rows
    col_first = (jnp.arange(dp_size, dtype=jnp.int32) * pair_size + pair_place) * shard_rows
    tile_rows = math.gcd(row_set.shape[1], 128)
    offsets = jnp.arange(shard_rows, dtype=jnp.int32)
    row_global = (row_first[:, None] + offsets[None, :]).reshape(-1)
    col_global = (col_first[:, None] + offsets[None, :]).reshape(-1)
    row_valid = row_global[None, :] < counts[:, None]
    col_valid = col_global[None, :] < counts[:, None]
    row_high, row_sum, col_high, col_sum = local_stats(
        row_set, col_set, row_global, col_valid, counts, score_scale, tile_rows
    )
    row_high, row_sum = joined((row_high, row_sum), "pair", merge_stats)
    col_high, col_sum = joined((col_high, col_sum), "dp", merge_stats)
    row_lse = jnp.where(row_valid, row_high + jnp.log(jnp.where(row_valid, row_sum, 1.0)), 0.0)
    col_lse = jnp.where(col_valid, col_high + jnp.log(jnp.where(col_valid, col_sum, 1.0)), 0.0)
    own_valid = own_first + offsets[None, :] < counts[:, None]
    row_own = lax.dynamic_slice_in_dim(row_lse, pair_place * shard_rows, shard_rows, 1)
    col_own = lax.dynamic_slice_in_dim(col_lse, dp_index * shard_rows, shard_rows, 1)
    positive = (
        jnp.sum(anchor.astype(jnp.float32) * partner.astype(jnp.float32), axis=2) * score_scale
    )
    loss_terms = jnp.where(own_valid, row_own + col_own - 2.0 * positive, 0.0)
    totals = lax.psum(jnp.sum(loss_terms, axis=1), ("dp", "pair"))
    loss_value = jnp.sum(totals / (2.0 * counts.astype(jnp.float32))) / pair_count
    anchor_outs = []
    partner_outs = []
    for pair_number in range(pair_count):
        grad_rows, grad_cols = pair_partials(
            row_set[pair_number],
            col_set[pair_number],
            row_global,
            col_valid[pair_number],
            counts[pair_number],
            row_lse[pair_number],
            col_lse[pair_number],
            pair_scale[pair_number],
            score_scale,
            tile_rows,
        )
        anchor_part = lax.psum_scatter(grad_rows, "pair", scatter_dimension=0, tiled=True)
        partner_part = lax.psum_scatter(grad_cols, "dp", scatter_dimension=0, tiled=True)
        own_term = pair_scale[pair_number] * score_scale
        keep_rows = own_valid[pair_number][:, None]
        anchor_outs.append(
            jnp.where(
                keep_rows, anchor_part - own_term * partner[pair_number].astype(jnp.float32), 0.0
            )
        )
        partner_outs.append(
            jnp.where(
                keep_rows, partner_part - own_term * anchor[pair_number].astype(jnp.float32), 0.0
            )
        )
    return (loss_value, jnp.stack(anchor_outs), jnp.stack(partner_outs))


def solution(mesh):
    in_specs = (P(None, ("dp", "pair"), None), P(None, ("dp", "pair"), None), P(), P())
    out_specs = (P(), P(None, ("dp", "pair"), None), P(None, ("dp", "pair"), None))
    return jax.shard_map(
        per_device, mesh=mesh, in_specs=in_specs, out_specs=out_specs, check_vma=False
    )
```

profile of v0, /device:TPU:0, one launch (start us, length us, event | category | flops | bytes accessed | tf_op | source)
XLA Modules:
  0.0 895.5 jit_solution(7603829063015780967)
XLA Ops:
  12.9 25.4 %all-gather.13.cloned.1.call-done = bf16[5,256,1024]{2,1,0:T(8,128)(2,1)} async-done(((bf16[5,32,1024]{2,1,0:T(8,128)(2,1)}), bf16[5,256,1024]{2,1,0:T(8,128)(2,1)}) %all-gather.13.cloned.1.call-update) | async-done | bytes 2621456 | tf_op jit(solution)/shard_map/all_gather | solution.py:169
  41.0 56.5 %all-gather.11.cloned.1.call-done = bf16[5,512,1024]{2,1,0:T(8,128)(2,1)} async-done(((bf16[5,32,1024]{2,1,0:T(8,128)(2,1)}), bf16[5,512,1024]{2,1,0:T(8,128)(2,1)}) %all-gather.11.cloned.1.call-update) | async-done | bytes 5242896 | tf_op jit(solution)/shard_map/all_gather | solution.py:168
  97.5 4.7 slice_bitcast_fusion
  102.2 24.6 %while.216 = (s32[]{:T(128)}, f32[512]{0:T(512)S(1)}, f32[512]{0:T(512)S(1)}, f32[256]{0:T(256)S(1)}, f32[256]{0:T(256)S(1)}, /*index=5*/s32[512]{0:T(512)S(1)},...) while((s32[]{:T(128)}, f32[512]{0:T(512)S(1)}, ...), condition=%wide.region_7.8_spmd.clone, body=%wide.region_0.7_spmd.clone.sunk | while | flops 67503496 | bytes 1064666 | solution.py:91
  126.8 24.1 %while.217 = (s32[]{:T(128)}, f32[512]{0:T(512)S(1)}, f32[512]{0:T(512)S(1)}, f32[256]{0:T(256)S(1)}, f32[256]{0:T(256)S(1)}, /*index=5*/s32[512]{0:T(512)S(1)},...) while((s32[]{:T(128)}, f32[512]{0:T(512)S(1)}, ...), condition=%wide.region_15.16_spmd.clone, body=%wide.region_8.15_spmd.clone.sunk | while | flops 67503496 | bytes 1064666 | solution.py:91
  151.0 23.7 %while.218 = (s32[]{:T(128)}, f32[512]{0:T(512)S(1)}, f32[512]{0:T(512)S(1)}, f32[256]{0:T(256)S(1)}, f32[256]{0:T(256)S(1)}, /*index=5*/s32[512]{0:T(512)S(1)},...) while((s32[]{:T(128)}, f32[512]{0:T(512)S(1)}, ...), condition=%wide.region_23.24_spmd.clone, body=%wide.region_16.23_spmd.clone.sunk | while | flops 67503496 | bytes 1064666 | solution.py:91
  174.6 24.5 %while.219 = (s32[]{:T(128)}, f32[512]{0:T(512)S(1)}, f32[512]{0:T(512)S(1)}, f32[256]{0:T(256)S(1)}, f32[256]{0:T(256)S(1)}, /*index=5*/s32[512]{0:T(512)S(1)},...) while((s32[]{:T(128)}, f32[512]{0:T(512)S(1)}, ...), condition=%wide.region_31.32_spmd.clone, body=%wide.region_24.31_spmd.clone.sunk | while | flops 67503496 | bytes 1064666 | solution.py:91
  199.2 19.3 %while.220 = (s32[]{:T(128)}, f32[512]{0:T(512)S(1)}, f32[512]{0:T(512)S(1)}, f32[256]{0:T(256)S(1)}, f32[256]{0:T(256)S(1)}, /*index=5*/s32[512]{0:T(512)S(1)},...) while((s32[]{:T(128)}, f32[512]{0:T(512)S(1)}, ...), condition=%wide.region_39.40_spmd.clone, body=%wide.region_32.39_spmd.clone.sunk | while | flops 67503496 | bytes 1065306 | solution.py:91
  218.5 12.8 %all-gather.6 = f32[8,5,256]{2,1,0:T(8,128)S(1)} all-gather(f32[1,5,256]{2,1,0:T(8,128)S(1)} %bitcast.287), channel_id=4, replica_groups=mesh['dp'=8,'pair'=16] {'dp'}, dimensions={0}, use_global_device_ids=true | all-gather | bytes 46080 | tf_op jit(solution)/shard_map/all_gather | solution.py:11
  231.3 12.7 %all-gather.7 = f32[8,5,256]{2,1,0:T(8,128)S(1)} all-gather(f32[1,5,256]{2,1,0:T(8,128)S(1)} %bitcast.288), channel_id=5, replica_groups=mesh['dp'=8,'pair'=16] {'dp'}, dimensions={0}, use_global_device_ids=true | all-gather | bytes 46080 | tf_op jit(solution)/shard_map/all_gather | solution.py:11
  244.3 23.4 %all-gather.4 = f32[16,5,512]{2,1,0:T(8,128)S(1)} all-gather(f32[1,5,512]{2,1,0:T(8,128)S(1)} %bitcast.275), channel_id=2, replica_groups=mesh['dp'=8,'pair'=16] {'pair'}, dimensions={0}, use_global_device_ids=true | all-gather | bytes 174080 | tf_op jit(solution)/shard_map/all_gather | solution.py:11
  267.8 21.6 %all-gather.5 = f32[16,5,512]{2,1,0:T(8,128)S(1)} all-gather(f32[1,5,512]{2,1,0:T(8,128)S(1)} %bitcast.276), channel_id=3, replica_groups=mesh['dp'=8,'pair'=16] {'pair'}, dimensions={0}, use_global_device_ids=true | all-gather | bytes 174080 | tf_op jit(solution)/shard_map/all_gather | solution.py:11
  290.1 11.4 %while.214 = (s32[]{:T(128)}, f32[5,512]{1,0:T(8,128)S(1)}, f32[5,512]{1,0:T(8,128)S(1)}, f32[16,5,512]{2,1,0:T(8,128)S(1)}, f32[16,5,512]{2,1,0:T(8,128)}, /*index=5*/s32[]{:T(128)}, s32[]{:T(128)}, s32[]{:T(128)}) while((s32[]{:T(128)}, f32[5,512]{1,0:T(8,128)S(1)}, f32[5,512]{1,0:T(8,128)S(1)}, f32[16,5,512]{2,1,0:T(8,128)S(1)}, ...), condition=%wide.region_41.42_spmd, body=%wide.region_40.41_spmd.sunk | while | flops 15365 | bytes 61571 | solution.py:16
  303.3 36.0 %while.221 = (s32[]{:T(128)}, f32[512,1024]{1,0:T(8,128)}, f32[256,1024]{1,0:T(8,128)}, s32[512]{0:T(512)S(1)}, s32[]{:T(128)}, /*index=5*/f32[]{:T(128)}, pred[...) while((s32[]{:T(128)}, f32[512,1024]{1,0:T(8,128)}, ...), condition=%wide.region_51.52_spmd.clone, body=%wide.region_48.51_spmd.clone.sunk | while | flops 202539136 | bytes 7542142 | solution.py:157
  304.0 5.3 conditional.35
  312.1 5.3 conditional.35
  321.4 5.4 conditional.35
  330.7 5.4 conditional.35
  341.5 32.1 %while.222 = (s32[]{:T(128)}, f32[512,1024]{1,0:T(8,128)}, f32[256,1024]{1,0:T(8,128)}, s32[512]{0:T(512)S(1)}, s32[]{:T(128)}, /*index=5*/f32[]{:T(128)}, pred[...) while((s32[]{:T(128)}, f32[512,1024]{1,0:T(8,128)}, ...), condition=%wide.region_56.57_spmd.clone, body=%wide.region_53.56_spmd.clone.sunk | while | flops 202539136 | bytes 7542142 | solution.py:157
  342.3 4.3 conditional.36
  349.4 4.3 conditional.36
  375.9 31.4 %while.223 = (s32[]{:T(128)}, f32[512,1024]{1,0:T(8,128)}, f32[256,1024]{1,0:T(8,128)}, s32[512]{0:T(512)S(1)}, s32[]{:T(128)}, /*index=5*/f32[]{:T(128)}, pred[...) while((s32[]{:T(128)}, f32[512,1024]{1,0:T(8,128)}, ...), condition=%wide.region_61.62_spmd.clone, body=%wide.region_58.61_spmd.clone.sunk | while | flops 202539136 | bytes 7542142 | solution.py:157
  409.9 31.9 %while.224 = (s32[]{:T(128)}, f32[512,1024]{1,0:T(8,128)}, f32[256,1024]{1,0:T(8,128)}, s32[512]{0:T(512)S(1)}, s32[]{:T(128)}, /*index=5*/f32[]{:T(128)}, pred[...) while((s32[]{:T(128)}, f32[512,1024]{1,0:T(8,128)}, ...), condition=%wide.region_66.67_spmd.clone, body=%wide.region_63.66_spmd.clone.sunk | while | flops 202539136 | bytes 7542142 | solution.py:157
  444.0 24.4 %while.225 = (s32[]{:T(128)}, f32[512,1024]{1,0:T(8,128)}, f32[256,1024]{1,0:T(8,128)S(1)}, s32[512]{0:T(512)S(1)}, s32[]{:T(128)}, /*index=5*/f32[]{:T(128)}, p...) while((s32[]{:T(128)}, f32[512,1024]{1,0:T(8,128)}, ...), condition=%wide.region_71.72_spmd.clone, body=%wide.region_68.71_spmd.clone.sunk | while | flops 202539136 | bytes 7542142 | solution.py:157
  473.5 63.1 %psum.7 = f32[5]{0:T(128)S(1)} all-reduce(f32[5]{0:T(128)S(1)} %select_reduce_fusion), channel_id=1, replica_groups=mesh['dp'=8,'pair'=16] {'dp','pair'}, use_global_device_ids=true, to_apply=%region_46.47 | all-reduce | flops 5 | bytes 40 | tf_op jit(solution)/shard_map/psum | solution.py:192
  539.0 16.0 %reduce-scatter.13.cloned.1.call-done = f32[32,1024]{1,0:T(8,128)} async-done(((f32[512,1024]{1,0:T(8,128)}), f32[32,1024]{1,0:T(8,128)}) %reduce-scatter.13.cloned.1.call-update) | async-done | bytes 131088 | tf_op jit(solution)/shard_map/reduce_scatter | solution.py:209
  556.1 32.3 %reduce-scatter.25.cloned.1.call-done = f32[32,1024]{1,0:T(8,128)} async-done(((f32[256,1024]{1,0:T(8,128)}), f32[32,1024]{1,0:T(8,128)}) %reduce-scatter.25.cloned.1.call-update) | async-done | bytes 131088 | tf_op jit(solution)/shard_map/reduce_scatter | solution.py:210
  588.4 76.7 %reduce-scatter.15.cloned.1.call-done = f32[32,1024]{1,0:T(8,128)} async-done(((f32[512,1024]{1,0:T(8,128)}), f32[32,1024]{1,0:T(8,128)}) %reduce-scatter.15.cloned.1.call-update) | async-done | bytes 131088 | tf_op jit(solution)/shard_map/reduce_scatter | solution.py:209
  666.2 32.4 %reduce-scatter.27.cloned.1.call-done = f32[32,1024]{1,0:T(8,128)} async-done(((f32[256,1024]{1,0:T(8,128)}), f32[32,1024]{1,0:T(8,128)}) %reduce-scatter.27.cloned.1.call-update) | async-done | bytes 131088 | tf_op jit(solution)/shard_map/reduce_scatter | solution.py:210
  698.6 76.9 %reduce-scatter.17.cloned.1.call-done = f32[32,1024]{1,0:T(8,128)} async-done(((f32[512,1024]{1,0:T(8,128)}), f32[32,1024]{1,0:T(8,128)}) %reduce-scatter.17.cloned.1.call-update) | async-done | bytes 131088 | tf_op jit(solution)/shard_map/reduce_scatter | solution.py:209
  776.6 32.3 %reduce-scatter.29.cloned.1.call-done = f32[32,1024]{1,0:T(8,128)} async-done(((f32[256,1024]{1,0:T(8,128)}), f32[32,1024]{1,0:T(8,128)}) %reduce-scatter.29.cloned.1.call-update) | async-done | bytes 131088 | tf_op jit(solution)/shard_map/reduce_scatter | solution.py:210
  808.8 76.5 %reduce-scatter.19.cloned.1.call-done = f32[32,1024]{1,0:T(8,128)} async-done(((f32[512,1024]{1,0:T(8,128)}), f32[32,1024]{1,0:T(8,128)}) %reduce-scatter.19.cloned.1.call-update) | async-done | bytes 131088 | tf_op jit(solution)/shard_map/reduce_scatter | solution.py:209
  (504 shorter events, 396.2 us)
Async XLA Ops:
  7.2 31.1 %all-gather.13.cloned.1.call-start = ((), (), s32[]{:S(2)}) async-start(), calls=%async_computation.11 | async-start | bytes 2949120 | tf_op jit(solution)/shard_map/all_gather | solution.py:169
  7.9 89.6 %all-gather.11.cloned.1.call-start = ((), (), s32[]{:S(2)}) async-start(), calls=%async_computation.10 | async-start | bytes 5570560 | tf_op jit(solution)/shard_map/all_gather | solution.py:168
  8.6 529.2 %reduce-scatter.21.cloned.1.call-start = ((), (), s32[]{:S(2)}) async-start(), calls=%async_computation.17 | async-start | bytes 1179648 | tf_op jit(solution)/shard_map/reduce_scatter | solution.py:210
  218.4 84.9 %copy-start.1 = (bf16[512,1024]{1,0:T(8,128)(2,1)}, bf16[512,1024]{1,0:T(8,128)(2,1)S(1)}, u32[]{:S(2)}) copy-start(bf16[512,1024]{1,0:T(8,128)(2,1)S(1)} %get-tuple-element.4396) | copy-start | bytes 3145732
  218.4 83.0 %copy-start.5 = (s32[5]{0:T(128)S(1)}, s32[5]{0:T(128)}, u32[]{:S(2)}) copy-start(s32[5]{0:T(128)} %param.50) | copy-start | bytes 64
  289.3 0.7 copy-start.4
  339.3 198.6 %reduce-scatter.11.cloned.1.call-start = ((), (), s32[]{:S(2)}) async-start(), calls=%async_computation.12 | async-start | bytes 2228224 | tf_op jit(solution)/shard_map/reduce_scatter | solution.py:209
  339.9 199.1 %reduce-scatter.23.cloned.1.call-start = ((), (), s32[]{:S(2)}) async-start(), calls=%async_computation.18 | async-start | bytes 1179648 | tf_op jit(solution)/shard_map/reduce_scatter | solution.py:210
  373.6 181.4 %reduce-scatter.13.cloned.1.call-start = ((), (), s32[]{:S(2)}) async-start(), calls=%async_computation.13 | async-start | bytes 2228224 | tf_op jit(solution)/shard_map/reduce_scatter | solution.py:209
  374.2 214.2 %reduce-scatter.25.cloned.1.call-start = ((), (), s32[]{:S(2)}) async-start(), calls=%async_computation.19 | async-start | bytes 1179648 | tf_op jit(solution)/shard_map/reduce_scatter | solution.py:210
  407.3 257.9 %reduce-scatter.15.cloned.1.call-start = ((), (), s32[]{:S(2)}) async-start(), calls=%async_computation.14 | async-start | bytes 2228224 | tf_op jit(solution)/shard_map/reduce_scatter | solution.py:209
  408.0 290.6 %reduce-scatter.27.cloned.1.call-start = ((), (), s32[]{:S(2)}) async-start(), calls=%async_computation.20 | async-start | bytes 1179648 | tf_op jit(solution)/shard_map/reduce_scatter | solution.py:210
  441.7 333.8 %reduce-scatter.17.cloned.1.call-start = ((), (), s32[]{:S(2)}) async-start(), calls=%async_computation.15 | async-start | bytes 2228224 | tf_op jit(solution)/shard_map/reduce_scatter | solution.py:209
  442.3 366.5 %reduce-scatter.29.cloned.1.call-start = ((), (), s32[]{:S(2)}) async-start(), calls=%async_computation.21 | async-start | bytes 1179648 | tf_op jit(solution)/shard_map/reduce_scatter | solution.py:210
  468.4 1.0 copy-start
  468.4 4.0 copy-start.2
  468.4 4.0 copy-start.3
  469.4 416.0 %reduce-scatter.19.cloned.1.call-start = ((), (), s32[]{:S(2)}) async-start(), calls=%async_computation.16 | async-start | bytes 2228224 | tf_op jit(solution)/shard_map/reduce_scatter | solution.py:209
  886.5 0.8 copy-start.6
  886.5 1.0 copy-start.7
Sparse Core Ops, SparseCore 0:
  9.7 28.5 all-gather.12
  40.4 57.0 all-gather.10
  339.4 28.6 reduce-scatter.20
  371.3 73.4 reduce-scatter.10
  447.2 30.9 reduce-scatter.22
  481.6 73.4 reduce-scatter.12
  557.5 30.8 reduce-scatter.24
  591.7 73.4 reduce-scatter.14
  667.6 30.9 reduce-scatter.26
  702.1 73.3 reduce-scatter.16
  777.9 30.9 reduce-scatter.28
  812.0 73.3 reduce-scatter.18
where the time goes:
time: 901 us; the launch traced here: 895 us
  waiting for transfers between devices  429 us (48%)
  blocking collectives  134 us (15%)
  other arithmetic  111 us (12%)
  matrix products  96.2 us (11%)
  local copies, waits for them, and re-layouts  63.8 us (7%)
  loops' own time  41.8 us (5%)
  between operations  19.5 us (2%)
    reduce_scatter x5, waiting for transfers between devices, per_device(): lax.psum_scatter(grad_rows, 'pair', scatter_dimension=0, tiled=True)  246 us
    reduce_scatter x5, waiting for transfers between devices, per_device(): lax.psum_scatter(grad_cols, 'dp', scatter_dimension=0, tiled=True)  97 us
    all_gather x4, blocking collectives, joined(): gathered = jax.tree.map(lambda a: lax.all_gather(a, axis), part)  70.5 us
    psum x1, blocking collectives, per_device(): totals = lax.psum(jnp.sum(loss_terms, axis=1), ('dp', 'pair'))  63.1 us
    dot_general x40, matrix products, block_scores(): jnp.einsum('rd,cd->rc', anchor_block, partner_rows, preferred_element_typ...  61.8 us
    all_gather x1, waiting for transfers between devices, per_device(): row_set = lax.all_gather(anchor, 'pair', axis=1, tiled=True)  56.5 us
    add x20, other arithmetic, pair_visit_block(): return (grad_rows, grad_cols + part_cols)  34.7 us
    dot_general x20, matrix products, pair_live_block(): jnp.einsum('rc,rd->cd', weights, anchor_block, preferred_element_type=jnp...  25.5 us
  transfers between devices with their start and end apart: 12, of which 9 were waited for; matrix products, arithmetic and copies ran while one was open for 13% of the time, Pallas kernels for 0%

commit v1 on v0

--- a/solution.py
+++ b/solution.py
@@ -166,7 +166,9 @@
     pair_place = lax.axis_index("pair")
     own_first = (dp_index * pair_size + pair_place) * shard_rows
     row_set = lax.all_gather(anchor, "pair", axis=1, tiled=True)
-    col_set = lax.all_gather(partner, "dp", axis=1, tiled=True)
+    col_set = jnp.concatenate(
+        lax.all_to_all(jnp.stack([partner] * lax.axis_size("dp")), "dp", 0, 0), axis=1
+    )
     row_first = (dp_index * pair_size + jnp.arange(pair_size, dtype=jnp.int32)) * shard_rows
     col_first = (jnp.arange(dp_size, dtype=jnp.int32) * pair_size + pair_place) * shard_rows
     tile_rows = math.gcd(row_set.shape[1], 128)

time: 901 us -> 872 us (0.968)
  waiting for transfers between devices: 429 us -> 395 us
    all_gather x1, waiting for transfers between devices: 56.5 us -> 16.7 us  [per_device(): row_set = lax.all_gather(anchor, 'pair', axis=1, tiled=True)]
    all_to_all x0 -> x1, waiting for transfers between devices: none -> 30.9 us  [per_device(): lax.all_to_all(jnp.stack([partner] * lax.axis_size('dp')), 'dp', 0, 0)]
    all_gather x1 -> x0, waiting for transfers between devices: 25.4 us -> none  [per_device(): col_set = lax.all_gather(partner, 'dp', axis=1, tiled=True)]
  transfers between devices with their start and end apart: 12 -> 12, of which waited for: 9 -> 9; matrix products, arithmetic and copies ran while one was open for 13% -> 14% of each run, Pallas kernels for 0% -> 0%
where the time goes in v1:
time: 872 us; the launch traced here: 867 us
  waiting for transfers between devices  395 us (45%)
  blocking collectives  133 us (15%)
  other arithmetic  110 us (13%)
  matrix products  96.2 us (11%)
  local copies, waits for them, and re-layouts  66.6 us (8%)
  loops' own time  41.8 us (5%)
  between operations  19.1 us (2%)
    reduce_scatter x5, waiting for transfers between devices, per_device(): lax.psum_scatter(grad_rows, 'pair', scatter_dimension=0, tiled=True)  246 us
    reduce_scatter x5, waiting for transfers between devices, per_device(): lax.psum_scatter(grad_cols, 'dp', scatter_dimension=0, tiled=True)  96.8 us
    all_gather x4, blocking collectives, joined(): gathered = jax.tree.map(lambda a: lax.all_gather(a, axis), part)  70.5 us
    psum x1, blocking collectives, per_device(): totals = lax.psum(jnp.sum(loss_terms, axis=1), ('dp', 'pair'))  62.9 us
    dot_general x40, matrix products, block_scores(): jnp.einsum('rd,cd->rc', anchor_block, partner_rows, preferred_element_typ...  61.8 us
    add x20, other arithmetic, pair_visit_block(): return (grad_rows, grad_cols + part_cols)  34.7 us
    all_to_all x1, waiting for transfers between devices, per_device(): lax.all_to_all(jnp.stack([partner] * lax.axis_size('dp')), 'dp', 0, 0)  30.9 us
    dot_general x20, matrix products, pair_live_block(): jnp.einsum('rc,rd->cd', weights, anchor_block, preferred_element_type=jnp...  25.5 us
  transfers between devices with their start and end apart: 12, of which 9 were waited for; matrix products, arithmetic and copies ran while one was open for 14% of the time, Pallas kernels for 0%

profile of v1, /device:TPU:0, one launch (start us, length us, event | category | flops | bytes accessed | tf_op | source)
XLA Modules:
  0.0 866.8 jit_solution(1955543401582813808)
XLA Ops:
  10.7 4.5 all-to-all-start
  17.1 30.9 %all-to-all-done = bf16[8,5,32,1024]{3,2,1,0:T(8,128)(2,1)S(1)} async-done(((bf16[8,5,32,1024]{3,2,1,0:T(8,128)(2,1)}), bf16[8,5,32,1024]{3,2,1,0:T(8,128)(2,1)S(1)}, u32[]{:S(2)}, u32[]{:S(2)}) %all-to-all-start) | async-done | bytes 2621472 | tf_op jit(solution)/shard_map/all_to_all | solution.py:170
  52.4 16.7 %all-gather.10.cloned.1.call-done = bf16[5,512,1024]{2,1,0:T(8,128)(2,1)} async-done(((bf16[5,32,1024]{2,1,0:T(8,128)(2,1)}), bf16[5,512,1024]{2,1,0:T(8,128)(2,1)}) %all-gather.10.cloned.1.call-update) | async-done | bytes 5242896 | tf_op jit(solution)/shard_map/all_gather | solution.py:168
  69.1 4.7 slice_bitcast_fusion
  73.8 24.6 %while.216 = (s32[]{:T(128)}, f32[512]{0:T(512)S(1)}, f32[512]{0:T(512)S(1)}, f32[256]{0:T(256)S(1)}, f32[256]{0:T(256)S(1)}, /*index=5*/s32[512]{0:T(512)S(1)},...) while((s32[]{:T(128)}, f32[512]{0:T(512)S(1)}, ...), condition=%wide.region_7.8_spmd.clone, body=%wide.region_0.7_spmd.clone.sunk | while | flops 67503496 | bytes 1064666 | solution.py:91
  98.4 24.1 %while.217 = (s32[]{:T(128)}, f32[512]{0:T(512)S(1)}, f32[512]{0:T(512)S(1)}, f32[256]{0:T(256)S(1)}, f32[256]{0:T(256)S(1)}, /*index=5*/s32[512]{0:T(512)S(1)},...) while((s32[]{:T(128)}, f32[512]{0:T(512)S(1)}, ...), condition=%wide.region_15.16_spmd.clone, body=%wide.region_8.15_spmd.clone.sunk | while | flops 67503496 | bytes 1064666 | solution.py:91
  122.6 23.7 %while.218 = (s32[]{:T(128)}, f32[512]{0:T(512)S(1)}, f32[512]{0:T(512)S(1)}, f32[256]{0:T(256)S(1)}, f32[256]{0:T(256)S(1)}, /*index=5*/s32[512]{0:T(512)S(1)},...) while((s32[]{:T(128)}, f32[512]{0:T(512)S(1)}, ...), condition=%wide.region_23.24_spmd.clone, body=%wide.region_16.23_spmd.clone.sunk | while | flops 67503496 | bytes 1064666 | solution.py:91
  146.3 24.5 %while.219 = (s32[]{:T(128)}, f32[512]{0:T(512)S(1)}, f32[512]{0:T(512)S(1)}, f32[256]{0:T(256)S(1)}, f32[256]{0:T(256)S(1)}, /*index=5*/s32[512]{0:T(512)S(1)},...) while((s32[]{:T(128)}, f32[512]{0:T(512)S(1)}, ...), condition=%wide.region_31.32_spmd.clone, body=%wide.region_24.31_spmd.clone.sunk | while | flops 67503496 | bytes 1064666 | solution.py:91
  170.8 19.3 %while.220 = (s32[]{:T(128)}, f32[512]{0:T(512)S(1)}, f32[512]{0:T(512)S(1)}, f32[256]{0:T(256)S(1)}, f32[256]{0:T(256)S(1)}, /*index=5*/s32[512]{0:T(512)S(1)},...) while((s32[]{:T(128)}, f32[512]{0:T(512)S(1)}, ...), condition=%wide.region_39.40_spmd.clone, body=%wide.region_32.39_spmd.clone.sunk | while | flops 67503496 | bytes 1065306 | solution.py:91
  190.1 12.8 %all-gather.6 = f32[8,5,256]{2,1,0:T(8,128)S(1)} all-gather(f32[1,5,256]{2,1,0:T(8,128)S(1)} %bitcast.288), channel_id=4, replica_groups=mesh['dp'=8,'pair'=16] {'dp'}, dimensions={0}, use_global_device_ids=true | all-gather | bytes 46080 | tf_op jit(solution)/shard_map/all_gather | solution.py:11
  202.9 12.7 %all-gather.7 = f32[8,5,256]{2,1,0:T(8,128)S(1)} all-gather(f32[1,5,256]{2,1,0:T(8,128)S(1)} %bitcast.289), channel_id=5, replica_groups=mesh['dp'=8,'pair'=16] {'dp'}, dimensions={0}, use_global_device_ids=true | all-gather | bytes 46080 | tf_op jit(solution)/shard_map/all_gather | solution.py:11
  216.0 23.4 %all-gather.4 = f32[16,5,512]{2,1,0:T(8,128)S(1)} all-gather(f32[1,5,512]{2,1,0:T(8,128)S(1)} %bitcast.276), channel_id=2, replica_groups=mesh['dp'=8,'pair'=16] {'pair'}, dimensions={0}, use_global_device_ids=true | all-gather | bytes 174080 | tf_op jit(solution)/shard_map/all_gather | solution.py:11
  239.4 21.6 %all-gather.5 = f32[16,5,512]{2,1,0:T(8,128)S(1)} all-gather(f32[1,5,512]{2,1,0:T(8,128)S(1)} %bitcast.277), channel_id=3, replica_groups=mesh['dp'=8,'pair'=16] {'pair'}, dimensions={0}, use_global_device_ids=true | all-gather | bytes 174080 | tf_op jit(solution)/shard_map/all_gather | solution.py:11
  261.7 11.4 %while.214 = (s32[]{:T(128)}, f32[5,512]{1,0:T(8,128)S(1)}, f32[5,512]{1,0:T(8,128)S(1)}, f32[16,5,512]{2,1,0:T(8,128)S(1)}, f32[16,5,512]{2,1,0:T(8,128)}, /*index=5*/s32[]{:T(128)}, s32[]{:T(128)}, s32[]{:T(128)}) while((s32[]{:T(128)}, f32[5,512]{1,0:T(8,128)S(1)}, f32[5,512]{1,0:T(8,128)S(1)}, f32[16,5,512]{2,1,0:T(8,128)S(1)}, ...), condition=%wide.region_41.42_spmd, body=%wide.region_40.41_spmd.sunk | while | flops 15365 | bytes 61571 | solution.py:16
  274.9 36.0 %while.221 = (s32[]{:T(128)}, f32[512,1024]{1,0:T(8,128)}, f32[256,1024]{1,0:T(8,128)}, s32[512]{0:T(512)S(1)}, s32[]{:T(128)}, /*index=5*/f32[]{:T(128)}, pred[...) while((s32[]{:T(128)}, f32[512,1024]{1,0:T(8,128)}, ...), condition=%wide.region_51.52_spmd.clone, body=%wide.region_48.51_spmd.clone.sunk | while | flops 202539136 | bytes 7542142 | solution.py:157
  275.6 5.4 conditional.35
  283.7 5.4 conditional.35
  293.0 5.3 conditional.35
  302.3 5.4 conditional.35
  313.3 32.1 %while.222 = (s32[]{:T(128)}, f32[512,1024]{1,0:T(8,128)}, f32[256,1024]{1,0:T(8,128)}, s32[512]{0:T(512)S(1)}, s32[]{:T(128)}, /*index=5*/f32[]{:T(128)}, pred[...) while((s32[]{:T(128)}, f32[512,1024]{1,0:T(8,128)}, ...), condition=%wide.region_56.57_spmd.clone, body=%wide.region_53.56_spmd.clone.sunk | while | flops 202539136 | bytes 7542142 | solution.py:157
  329.5 4.3 conditional.36
  347.8 31.4 %while.223 = (s32[]{:T(128)}, f32[512,1024]{1,0:T(8,128)}, f32[256,1024]{1,0:T(8,128)}, s32[512]{0:T(512)S(1)}, s32[]{:T(128)}, /*index=5*/f32[]{:T(128)}, pred[...) while((s32[]{:T(128)}, f32[512,1024]{1,0:T(8,128)}, ...), condition=%wide.region_61.62_spmd.clone, body=%wide.region_58.61_spmd.clone.sunk | while | flops 202539136 | bytes 7542142 | solution.py:157
  381.7 31.8 %while.224 = (s32[]{:T(128)}, f32[512,1024]{1,0:T(8,128)}, f32[256,1024]{1,0:T(8,128)}, s32[512]{0:T(512)S(1)}, s32[]{:T(128)}, /*index=5*/f32[]{:T(128)}, pred[...) while((s32[]{:T(128)}, f32[512,1024]{1,0:T(8,128)}, ...), condition=%wide.region_66.67_spmd.clone, body=%wide.region_63.66_spmd.clone.sunk | while | flops 202539136 | bytes 7542142 | solution.py:157
  416.0 24.4 %while.225 = (s32[]{:T(128)}, f32[512,1024]{1,0:T(8,128)}, f32[256,1024]{1,0:T(8,128)S(1)}, s32[512]{0:T(512)S(1)}, s32[]{:T(128)}, /*index=5*/f32[]{:T(128)}, p...) while((s32[]{:T(128)}, f32[512,1024]{1,0:T(8,128)}, ...), condition=%wide.region_71.72_spmd.clone, body=%wide.region_68.71_spmd.clone.sunk | while | flops 202539136 | bytes 7542142 | solution.py:157
  445.6 62.9 %psum.7 = f32[5]{0:T(128)S(1)} all-reduce(f32[5]{0:T(128)S(1)} %select_reduce_fusion), channel_id=1, replica_groups=mesh['dp'=8,'pair'=16] {'dp','pair'}, use_global_device_ids=true, to_apply=%region_46.47 | all-reduce | flops 5 | bytes 40 | tf_op jit(solution)/shard_map/psum | solution.py:194
  510.9 16.0 %reduce-scatter.13.cloned.1.call-done = f32[32,1024]{1,0:T(8,128)} async-done(((f32[512,1024]{1,0:T(8,128)}), f32[32,1024]{1,0:T(8,128)}) %reduce-scatter.13.cloned.1.call-update) | async-done | bytes 131088 | tf_op jit(solution)/shard_map/reduce_scatter | solution.py:211
  527.9 32.2 %reduce-scatter.25.cloned.1.call-done = f32[32,1024]{1,0:T(8,128)} async-done(((f32[256,1024]{1,0:T(8,128)}), f32[32,1024]{1,0:T(8,128)}) %reduce-scatter.25.cloned.1.call-update) | async-done | bytes 131088 | tf_op jit(solution)/shard_map/reduce_scatter | solution.py:212
  560.1 76.6 %reduce-scatter.15.cloned.1.call-done = f32[32,1024]{1,0:T(8,128)} async-done(((f32[512,1024]{1,0:T(8,128)}), f32[32,1024]{1,0:T(8,128)}) %reduce-scatter.15.cloned.1.call-update) | async-done | bytes 131088 | tf_op jit(solution)/shard_map/reduce_scatter | solution.py:211
  637.8 32.4 %reduce-scatter.27.cloned.1.call-done = f32[32,1024]{1,0:T(8,128)} async-done(((f32[256,1024]{1,0:T(8,128)}), f32[32,1024]{1,0:T(8,128)}) %reduce-scatter.27.cloned.1.call-update) | async-done | bytes 131088 | tf_op jit(solution)/shard_map/reduce_scatter | solution.py:212
  670.2 77.0 %reduce-scatter.17.cloned.1.call-done = f32[32,1024]{1,0:T(8,128)} async-done(((f32[512,1024]{1,0:T(8,128)}), f32[32,1024]{1,0:T(8,128)}) %reduce-scatter.17.cloned.1.call-update) | async-done | bytes 131088 | tf_op jit(solution)/shard_map/reduce_scatter | solution.py:211
  748.2 32.2 %reduce-scatter.29.cloned.1.call-done = f32[32,1024]{1,0:T(8,128)} async-done(((f32[256,1024]{1,0:T(8,128)}), f32[32,1024]{1,0:T(8,128)}) %reduce-scatter.29.cloned.1.call-update) | async-done | bytes 131088 | tf_op jit(solution)/shard_map/reduce_scatter | solution.py:212
  780.4 76.6 %reduce-scatter.19.cloned.1.call-done = f32[32,1024]{1,0:T(8,128)} async-done(((f32[512,1024]{1,0:T(8,128)}), f32[32,1024]{1,0:T(8,128)}) %reduce-scatter.19.cloned.1.call-update) | async-done | bytes 131088 | tf_op jit(solution)/shard_map/reduce_scatter | solution.py:211
  (508 shorter events, 402.4 us)
Async XLA Ops:
  7.2 62.0 %all-gather.10.cloned.1.call-start = ((), (), s32[]{:S(2)}) async-start(), calls=%async_computation.11 | async-start | bytes 5570560 | tf_op jit(solution)/shard_map/all_gather | solution.py:168
  10.7 5.0 copy-start.6
  10.7 5.7 copy-start.9
  10.7 37.3 %all-to-all-start = ((bf16[8,5,32,1024]{3,2,1,0:T(8,128)(2,1)}), bf16[8,5,32,1024]{3,2,1,0:T(8,128)(2,1)S(1)}, u32[]{:S(2)}, u32[]{:S(2)}) async-start(bf16[8,5,32,1024]{3,2,1,0:T(8,128)(2,1)} %stack.119), calls=%async_computation | async-start | bytes 5242880 | tf_op jit(solution)/shard_map/all_to_all | solution.py:170
  15.2 494.6 %reduce-scatter.21.cloned.1.call-start = ((), (), s32[]{:S(2)}) async-start(), calls=%async_computation.17 | async-start | bytes 1179648 | tf_op jit(solution)/shard_map/reduce_scatter | solution.py:212
  48.0 1.5 copy-start.2
  190.1 84.8 %copy-start.1 = (bf16[512,1024]{1,0:T(8,128)(2,1)}, bf16[512,1024]{1,0:T(8,128)(2,1)S(1)}, u32[]{:S(2)}) copy-start(bf16[512,1024]{1,0:T(8,128)(2,1)S(1)} %get-tuple-element.4395) | copy-start | bytes 3145732
  261.0 0.7 copy-start.5
  310.9 198.9 %reduce-scatter.11.cloned.1.call-start = ((), (), s32[]{:S(2)}) async-start(), calls=%async_computation.12 | async-start | bytes 2228224 | tf_op jit(solution)/shard_map/reduce_scatter | solution.py:211
  311.7 199.2 %reduce-scatter.23.cloned.1.call-start = ((), (), s32[]{:S(2)}) async-start(), calls=%async_computation.18 | async-start | bytes 1179648 | tf_op jit(solution)/shard_map/reduce_scatter | solution.py:212
  345.4 181.4 %reduce-scatter.13.cloned.1.call-start = ((), (), s32[]{:S(2)}) async-start(), calls=%async_computation.13 | async-start | bytes 2228224 | tf_op jit(solution)/shard_map/reduce_scatter | solution.py:211
  346.0 214.1 %reduce-scatter.25.cloned.1.call-start = ((), (), s32[]{:S(2)}) async-start(), calls=%async_computation.19 | async-start | bytes 1179648 | tf_op jit(solution)/shard_map/reduce_scatter | solution.py:212
  379.2 257.5 %reduce-scatter.15.cloned.1.call-start = ((), (), s32[]{:S(2)}) async-start(), calls=%async_computation.14 | async-start | bytes 2228224 | tf_op jit(solution)/shard_map/reduce_scatter | solution.py:211
  380.0 290.2 %reduce-scatter.27.cloned.1.call-start = ((), (), s32[]{:S(2)}) async-start(), calls=%async_computation.20 | async-start | bytes 1179648 | tf_op jit(solution)/shard_map/reduce_scatter | solution.py:212
  413.5 333.7 %reduce-scatter.17.cloned.1.call-start = ((), (), s32[]{:S(2)}) async-start(), calls=%async_computation.15 | async-start | bytes 2228224 | tf_op jit(solution)/shard_map/reduce_scatter | solution.py:211
  414.3 366.2 %reduce-scatter.29.cloned.1.call-start = ((), (), s32[]{:S(2)}) async-start(), calls=%async_computation.21 | async-start | bytes 1179648 | tf_op jit(solution)/shard_map/reduce_scatter | solution.py:212
  440.4 1.0 copy-start
  440.4 4.1 copy-start.3
  440.4 4.1 copy-start.4
  441.4 415.7 %reduce-scatter.19.cloned.1.call-start = ((), (), s32[]{:S(2)}) async-start(), calls=%async_computation.16 | async-start | bytes 2228224 | tf_op jit(solution)/shard_map/reduce_scatter | solution.py:211
  858.1 0.8 copy-start.7
  858.1 1.0 copy-start.8
Sparse Core Ops, SparseCore 0:
  10.1 58.9 all-gather.9
  311.1 28.6 reduce-scatter.20
  343.0 73.5 reduce-scatter.10
  419.0 30.9 reduce-scatter.22
  453.5 73.3 reduce-scatter.12
  529.1 30.9 reduce-scatter.24
  563.4 73.2 reduce-scatter.14
  639.2 30.9 reduce-scatter.26
  673.8 73.2 reduce-scatter.16
  749.4 30.9 reduce-scatter.28
  783.7 73.2 reduce-scatter.18
